TPU v7x, 32 devices: a whole 2x2x4 slice. The times are simulated.
32 devices in a mesh: group: 2 (over y), seq: 4 (over z), batch: 2 (over x), mp: 2 (over core).
Axes of the slice: x: 2, y: 2, z: 4, core: 2. Of those that a mesh axis runs over, the one named last changes fastest.
Arguments:
- features: bfloat16 [4, 512, 384], P(('group', 'batch'), 'seq'), parts along dimension 0, may hold values from -6 to 6
- noise: float32 [4, 512, 384], P(('group', 'batch'), 'seq'), parts along dimension 0, may hold values from -3 to 3
- conv_weight: bfloat16 [5, 384, 768], P(None, 'seq', 'mp'), may hold values from -0.125 to 0.125
- conv_bias: float32 [768], P('mp'), may hold values from -3 to 3
- norm_gain: float32 [768], replicated, may hold values from 0.25 to 1.75
- qkv_weight: bfloat16 [3, 768, 768], P(None, 'seq', 'mp'), may hold values from -1.010363 to 1.010363
- out_weight: bfloat16 [768, 768], P('mp', 'seq'), may hold values from -0.21875 to 0.21875
Outputs:
- block_out: bfloat16 [4, 256, 768], P(('group', 'batch'), 'seq', 'mp'), parts along dimension 0
- new_noise: float32 [4, 512, 384], P(('group', 'batch'), 'seq'), parts along dimension 0
There are 2 independent parts, one for each index of `group`. A program takes and returns all parts, laid end to end along the dimension named above; an argument that names none is the same for every part. Nothing has to cross between parts.
All inputs are finite; a program needn't handle non-finite values.
Results may differ from a plain program's by a relative error of at most 0.014.
Values may be sent and summed in bfloat16 or wider, within the bound.
No kernel may reach another device: no remote copies, remote signals or barrier semaphores. Data moves between devices by JAX's collectives and lax.ppermute only.
A program may use at most 64 MiB of HBM per device.

v0:
```python
import jax
import jax.numpy as jnp
from jax import lax
from jax.sharding import PartitionSpec as P

F = 768
HD = 96
KW = 5
step_size = 0.5
epsilon = 1e-06


def with_halo(cells, sides, width):
    for axis, dim in sides:
        count = lax.axis_size(axis)
        ends = count - 1
        head = lax.slice_in_dim(cells, 0, width, axis=dim)
        tail = lax.slice_in_dim(cells, cells.shape[dim] - width, cells.shape[dim], axis=dim)
        cells = jnp.concatenate(
            [
                lax.ppermute(tail, axis, [(i, (i + 1) % count) for i in range(ends)]),
                cells,
                lax.ppermute(head, axis, [((i + 1) % count, i) for i in range(ends)]),
            ],
            axis=dim,
        )
    return cells


def attend_rows(query, keys, values):
    key_total = keys.shape[0]
    block_len = min(512, key_total)
    head_size = keys.shape[1]
    score_scale = head_size ** (-0.5)
    key_blocks = keys.reshape(key_total // block_len, block_len, head_size)
    value_blocks = values.reshape(key_total // block_len, block_len, head_size)
    query_count = query.shape[0]

    def find_top(carry, key_block):
        row_top, row_mass = carry
        scores = jnp.dot(query, key_block.T, preferred_element_type=jnp.float32) * score_scale
        new_top = jnp.maximum(row_top, jnp.max(scores, axis=1))
        row_mass = row_mass * jnp.exp(row_top - new_top) + jnp.sum(
            jnp.exp(scores - new_top[:, None]), axis=1
        )
        return ((new_top, row_mass), None)

    start_top = jnp.full((query_count,), -1e30, jnp.float32)
    (row_top, row_mass), _ = lax.scan(
        find_top, (start_top, jnp.zeros((query_count,), jnp.float32)), key_blocks
    )
    log_mass = row_top + jnp.log(row_mass)

    def collect(running, blocks):
        key_block, value_block = blocks
        scores = jnp.dot(query, key_block.T, preferred_element_type=jnp.float32) * score_scale
        soft_weights = jnp.exp(scores - log_mass[:, None]).astype(jnp.bfloat16)
        return (
            running + jnp.dot(soft_weights, value_block, preferred_element_type=jnp.float32),
            None,
        )

    running, _ = lax.scan(
        collect, jnp.zeros((query_count, head_size), jnp.float32), (key_blocks, value_blocks)
    )
    return (running.astype(jnp.bfloat16), log_mass)


def attend_back(query, keys, values, attended, log_mass, out_grad):
    key_total = keys.shape[0]
    block_len = min(512, key_total)
    head_size = keys.shape[1]
    score_scale = head_size ** (-0.5)
    key_blocks = keys.reshape(key_total // block_len, block_len, head_size)
    value_blocks = values.reshape(key_total // block_len, block_len, head_size)
    row_dot = jnp.sum(out_grad.astype(jnp.float32) * attended.astype(jnp.float32), axis=1)

    def step_back(query_acc, blocks):
        key_block, value_block = blocks
        scores = jnp.dot(query, key_block.T, preferred_element_type=jnp.float32) * score_scale
        exp_weights = jnp.exp(scores - log_mass[:, None])
        value_part = jnp.einsum(
            "qk,qd->kd",
            exp_weights.astype(jnp.bfloat16),
            out_grad,
            preferred_element_type=jnp.float32,
        )
        prob_grad = jnp.dot(out_grad, value_block.T, preferred_element_type=jnp.float32)
        score_grad = (exp_weights * (prob_grad - row_dot[:, None])).astype(jnp.bfloat16)
        query_acc = (
            query_acc
            + jnp.dot(score_grad, key_block, preferred_element_type=jnp.float32) * score_scale
        )
        key_part = (
            jnp.einsum("qk,qd->kd", score_grad, query, preferred_element_type=jnp.float32)
            * score_scale
        )
        return (query_acc, jnp.concatenate([key_part, value_part], axis=1))

    query_grad, keyval_parts = lax.scan(
        step_back, jnp.zeros((query.shape[0], head_size), jnp.float32), (key_blocks, value_blocks)
    )
    return (query_grad, keyval_parts.reshape(key_total, 2 * head_size))


def forward(stack, conv_weight, conv_bias, norm_gain, qkv_weight, out_weight):
    pass_count, positions, channels = stack.shape
    reach = KW // 2
    half_width = conv_weight.shape[2]
    padded_input = with_halo(stack, (("seq", 1),), reach)
    running = jnp.zeros((pass_count, positions, half_width), jnp.float32)
    piece = lax.all_gather(conv_weight, "seq", axis=1, tiled=True)
    for offset in range(piece.shape[0]):
        running = running + jnp.einsum(
            "ptc,cf->ptf",
            padded_input[:, offset : offset + positions],
            piece[offset],
            preferred_element_type=jnp.float32,
        )
    pre_act = running + conv_bias
    paired = jax.nn.gelu(pre_act).reshape(pass_count, positions // 2, 2, half_width)
    pooled = (0.5 * (paired[:, :, 0] + paired[:, :, 1])).astype(jnp.bfloat16)
    pooled_wide = lax.optimization_barrier(pooled).astype(jnp.float32)
    whole = lax.all_gather(pooled, "mp", axis=2, tiled=True)
    whole_wide = whole.astype(jnp.float32)
    row_scale = lax.rsqrt(jnp.mean(whole_wide * whole_wide, axis=2, keepdims=True) + epsilon)
    normed = (whole_wide * row_scale * norm_gain).astype(jnp.bfloat16)
    rows = positions // 2
    proj_width = qkv_weight.shape[2]
    projected = jnp.einsum(
        "prf,jfh->jprh",
        normed,
        lax.all_gather(qkv_weight, "seq", axis=1, tiled=True),
        preferred_element_type=jnp.float32,
    ).astype(jnp.bfloat16)
    head_size = HD
    head_count = proj_width // head_size
    devices = lax.axis_size("seq")
    query_groups = devices // head_count
    sub_rows = rows // query_groups
    query_send = (
        projected[0]
        .reshape(pass_count, query_groups, sub_rows, head_count, head_size)
        .transpose(3, 1, 0, 2, 4)
        .reshape(devices, pass_count, sub_rows * head_size)
    )
    keyval = jnp.concatenate(
        [
            projected[1].reshape(pass_count, rows, head_count, head_size),
            projected[2].reshape(pass_count, rows, head_count, head_size),
        ],
        axis=3,
    )
    keyval_flat = keyval.transpose(2, 0, 1, 3).reshape(
        head_count, 1, pass_count, rows * 2 * head_size
    )
    keyval_send = jnp.broadcast_to(
        keyval_flat, (head_count, query_groups, pass_count, rows * 2 * head_size)
    ).reshape(devices, pass_count, rows * 2 * head_size)
    query_in, keyval_in = (
        lax.all_to_all(query_send, "seq", split_axis=0, concat_axis=2, tiled=True),
        lax.all_to_all(keyval_send, "seq", split_axis=0, concat_axis=2, tiled=True),
    )
    query_heads = query_in.reshape(pass_count, devices * sub_rows, head_size)
    keyval_heads = keyval_in.reshape(pass_count, devices * rows, 2 * head_size)
    outputs = []
    masses = []
    for index in range(pass_count):
        out_now, mass_now = attend_rows(
            query_heads[index],
            keyval_heads[index, :, :head_size],
            keyval_heads[index, :, head_size:],
        )
        outputs.append(out_now)
        masses.append(mass_now)
    attended_heads = jnp.stack(outputs)
    log_mass = jnp.stack(masses)
    out_send = attended_heads.reshape(pass_count, devices, sub_rows * head_size).transpose(1, 0, 2)
    out_back = lax.all_to_all(out_send, "seq", split_axis=0, concat_axis=0, tiled=True)
    attended = (
        out_back.reshape(head_count, query_groups, pass_count, sub_rows, head_size)
        .transpose(2, 1, 3, 0, 4)
        .reshape(pass_count, rows, proj_width)
    )
    terms = jnp.einsum(
        "prh,hf->prf",
        attended,
        lax.all_gather(out_weight, "seq", axis=1, tiled=True),
        preferred_element_type=jnp.float32,
    )
    mixed = (
        lax.psum_scatter(terms.astype(jnp.bfloat16), "mp", scatter_dimension=2, tiled=True).astype(
            jnp.float32
        )
        + pooled_wide
    )
    return (
        pre_act,
        pooled_wide,
        whole_wide,
        row_scale,
        query_heads,
        keyval_heads,
        attended_heads,
        log_mass,
        mixed,
    )


def shards(features, noise, conv_weight, conv_bias, norm_gain, qkv_weight, out_weight):
    clean = features[0]
    moved = (clean.astype(jnp.float32) + noise[0]).astype(jnp.bfloat16)
    joint = forward(
        jnp.stack([clean, moved]), conv_weight, conv_bias, norm_gain, qkv_weight, out_weight
    )
    clean_run = [item[0:1] for item in joint]
    moved_run = [item[1:2] for item in joint]
    (
        pre_act,
        pooled_wide,
        whole_wide,
        row_scale,
        query_heads,
        keyval_heads,
        attended_heads,
        log_mass,
        mixed,
    ) = [item[0] for item in moved_run]
    clean_mixed = clean_run[8][0]
    rows, half_width = pooled_wide.shape
    positions = pre_act.shape[0]
    proj_width = qkv_weight.shape[2]
    head_size = HD
    head_count = proj_width // head_size
    devices = lax.axis_size("seq")
    query_groups = devices // head_count
    sub_rows = rows // query_groups
    difference = mixed - clean_mixed
    difference_half = difference.astype(jnp.bfloat16)
    difference_whole = lax.all_gather(difference_half, "mp", axis=1, tiled=True)
    out_grad = jnp.einsum(
        "rf,hf->rh",
        difference_whole,
        lax.all_gather(out_weight, "seq", axis=1, tiled=True),
        preferred_element_type=jnp.float32,
    ).astype(jnp.bfloat16)
    grad_send = (
        out_grad.reshape(query_groups, sub_rows, head_count, head_size)
        .transpose(2, 0, 1, 3)
        .reshape(devices, sub_rows * head_size)
    )
    grad_in = lax.all_to_all(grad_send, "seq", split_axis=0, concat_axis=1, tiled=True)
    grad_heads = grad_in.reshape(devices * sub_rows, head_size)
    query_grad, keyval_grad = attend_back(
        query_heads,
        keyval_heads[:, :head_size],
        keyval_heads[:, head_size:],
        attended_heads,
        log_mass,
        grad_heads,
    )
    query_back, keyval_back = (
        lax.all_to_all(
            query_grad.reshape(devices, sub_rows * head_size).astype(jnp.bfloat16),
            "seq",
            split_axis=0,
            concat_axis=0,
            tiled=True,
        ).astype(jnp.float32),
        lax.all_to_all(
            keyval_grad.reshape(devices, rows * 2 * head_size).astype(jnp.bfloat16),
            "seq",
            split_axis=0,
            concat_axis=0,
            tiled=True,
        ).astype(jnp.float32),
    )
    query_rows = (
        query_back.reshape(head_count, query_groups, sub_rows, head_size)
        .transpose(1, 2, 0, 3)
        .reshape(rows, proj_width)
        .astype(jnp.bfloat16)
    )
    keyval_rows = jnp.sum(keyval_back.reshape(head_count, query_groups, rows, 2, head_size), axis=1)
    key_rows = (
        keyval_rows[:, :, 0].transpose(1, 0, 2).reshape(rows, proj_width).astype(jnp.bfloat16)
    )
    value_rows = (
        keyval_rows[:, :, 1].transpose(1, 0, 2).reshape(rows, proj_width).astype(jnp.bfloat16)
    )
    grads = jnp.stack([query_rows, key_rows, value_rows])
    normed_terms = jnp.einsum(
        "jrh,jfh->rf",
        grads,
        lax.all_gather(qkv_weight, "seq", axis=1, tiled=True),
        preferred_element_type=jnp.float32,
    )
    offset_mp = lax.axis_index("mp") * half_width
    gain_own = lax.dynamic_slice_in_dim(norm_gain, offset_mp, half_width, 0)
    normed_grad = lax.psum_scatter(
        normed_terms.astype(jnp.bfloat16), "mp", scatter_dimension=1, tiled=True
    ).astype(jnp.float32)
    weighted = lax.psum(jnp.sum(normed_grad * gain_own * pooled_wide, axis=1, keepdims=True), "mp")
    pooled_grad = (
        difference + row_scale * gain_own * normed_grad - pooled_wide * row_scale**3 * weighted / F
    )
    spread = jnp.broadcast_to((0.5 * pooled_grad)[:, None, :], (rows, 2, half_width)).reshape(
        positions, half_width
    )
    gelu_back = jax.vjp(jax.nn.gelu, pre_act)[1]
    pre_grad = gelu_back(spread)[0].astype(jnp.bfloat16)
    reach = KW // 2
    padded = with_halo(pre_grad, (("seq", 0),), reach)
    piece = lax.all_gather(conv_weight, "seq", axis=1, tiled=True)
    running = jnp.zeros((positions, piece.shape[1]), jnp.float32)
    for offset in range(piece.shape[0]):
        lower = 2 * reach - offset
        running = running + jnp.einsum(
            "tf,cf->tc",
            padded[lower : lower + positions],
            piece[offset],
            preferred_element_type=jnp.float32,
        )
    input_grad = lax.psum(running.astype(jnp.bfloat16), "mp").astype(jnp.float32)
    new_noise = noise[0] + step_size * input_grad * lax.rsqrt(
        jnp.mean(input_grad * input_grad, axis=1, keepdims=True) + epsilon
    )
    return (clean_mixed.astype(jnp.bfloat16)[None], new_noise[None])


def solution(mesh):
    return jax.shard_map(
        shards,
        mesh=mesh,
        in_specs=(
            P(("group", "batch"), "seq", None),
            P(("group", "batch"), "seq", None),
            P(None, "seq", "mp"),
            P("mp"),
            P(),
            P(None, "seq", "mp"),
            P("mp", "seq"),
        ),
        out_specs=(P(("group", "batch"), "seq", "mp"), P(("group", "batch"), "seq", None)),
        check_vma=False,
    )
```

profile of v0, /device:TPU:0, one launch (start us, length us, event | category | flops | bytes accessed | tf_op | source)
XLA Modules:
  0.0 244.7 jit_solution(5682853137255914638)
XLA Ops:
  10.4 4.9 %collective-permute-start = (bf16[2,2,384]{2,1,0:T(2,128)(2,1)S(1)}, bf16[2,2,384]{2,1,0:T(2,128)(2,1)S(1)}, u32[]{:S(2)}, u32[]{:S(2)}) collective-permute-start(bf16[2,2,384]{2,1,0:T(2,128)(2,1)S(1)} %get-tuple-element.88), channel_id=1, source_target_pairs={{0,4},{4,8},{8,12},{1,5},{5,9},{9,13},{2,6},{6,10},{10,14},{3,7},{... | collective-permute-start | bytes 9224 | tf_op jit(solution)/shard_map/ppermute | solution.py:21
  15.4 1.3 collective-permute-start.1
  16.7 4.2 %collective-permute-done.1 = bf16[2,2,384]{2,1,0:T(2,128)(2,1)S(1)} collective-permute-done((bf16[2,2,384]{2,1,0:T(2,128)(2,1)S(1)}, bf16[2,2,384]{2,1,0:T(2,128)(2,1)S(1)}, u32[]{:S(2)}, u32[]{:S(2)}) %collective-permute-start.1) | collective-permute-done | bytes 3104 | tf_op jit(solution)/shard_map/ppermute | solution.py:23
  20.9 26.7 %all-gather.4.cloned.1.call-done = bf16[5,384,384]{2,1,0:T(8,128)(2,1)} async-done(((bf16[5,96,384]{2,1,0:T(8,128)(2,1)}), bf16[5,384,384]{2,1,0:T(8,128)(2,1)}) %all-gather.4.cloned.1.call-update) | async-done | bytes 1474576 | tf_op jit(solution)/shard_map/all_gather | solution.py:112
  47.6 1.3 fusion.38
  51.9 1.9 all-gather
  54.0 34.5 %all-gather.6.cloned.1.call-done = bf16[3,768,384]{2,1,0:T(8,128)(2,1)} async-done(((bf16[3,192,384]{2,1,0:T(8,128)(2,1)}), bf16[3,768,384]{2,1,0:T(8,128)(2,1)}) %all-gather.6.cloned.1.call-update) | async-done | bytes 1769488 | tf_op jit(solution)/shard_map/all_gather | solution.py:133
  88.5 2.0 fusion.8
  91.5 3.3 %all-to-all-start = ((bf16[4,2,6144]{2,1,0:T(2,128)(2,1)}), bf16[4,2,6144]{2,1,0:T(2,128)(2,1)S(1)}, u32[]{:S(2)}, u32[]{:S(2)}) async-start(bf16[4,2,6144]{2,1,0:T(2,128)(2,1)} %reshape.242), calls=%async_computation | async-start | bytes 196608 | tf_op jit(solution)/shard_map/all_to_all | solution.py:161
  96.3 4.3 %all-to-all-done = bf16[4,2,6144]{2,1,0:T(2,128)(2,1)S(1)} async-done(((bf16[4,2,6144]{2,1,0:T(2,128)(2,1)}), bf16[4,2,6144]{2,1,0:T(2,128)(2,1)S(1)}, u32[]{:S(2)}, u32[]{:S(2)}) %all-to-all-start) | async-done | bytes 98336 | tf_op jit(solution)/shard_map/all_to_all | solution.py:161
  100.6 3.4 %all-to-all-start.1 = ((bf16[4,2,12288]{2,1,0:T(2,128)(2,1)}), bf16[4,2,12288]{2,1,0:T(2,128)(2,1)S(1)}, u32[]{:S(2)}, u32[]{:S(2)}) async-start(bf16[4,2,12288]{2,1,0:T(2,128)(2,1)} %reshape_reshape.4), calls=%async_computation.1 | async-start | bytes 393216 | tf_op jit(solution)/shard_map/all_to_all | solution.py:162
  104.6 5.5 %all-to-all-done.1 = bf16[4,2,12288]{2,1,0:T(2,128)(2,1)S(1)} async-done(((bf16[4,2,12288]{2,1,0:T(2,128)(2,1)}), bf16[4,2,12288]{2,1,0:T(2,128)(2,1)S(1)}, u32[]{:S(2)}, u32[]{:S(2)}) %all-to-all-start.1) | async-done | bytes 196640 | tf_op jit(solution)/shard_map/all_to_all | solution.py:162
  113.2 3.3 %all-to-all-start.2 = ((bf16[4,2,6144]{2,1,0:T(2,128)(2,1)}), bf16[4,2,6144]{2,1,0:T(2,128)(2,1)S(1)}, u32[]{:S(2)}, u32[]{:S(2)}) async-start(bf16[4,2,6144]{2,1,0:T(2,128)(2,1)} %copy.103), calls=%async_computation.2 | async-start | bytes 196608 | tf_op jit(solution)/shard_map/all_to_all | solution.py:179
  116.6 16.8 %all_gather.21 = bf16[384,768]{0,1:T(8,128)(2,1)S(1)} all-gather(bf16[384,192]{0,1:T(8,128)(2,1)S(1)} %copy-done.8), channel_id=1, replica_groups=mesh['group'=2,'seq'=4,'batch'=2,'mp'=2] {'seq'}, dimensions={1}, use_global_device_ids=true | all-gather | bytes 737280 | tf_op jit(solution)/shard_map/all_gather | solution.py:188
  137.8 5.3 %reduce-scatter.7.cloned.1.call-done = bf16[384,128]{1,0:T(8,128)(2,1)} async-done(((bf16[768,128]{1,0:T(8,128)(2,1)}), bf16[384,128]{1,0:T(8,128)(2,1)}) %reduce-scatter.7.cloned.1.call-update) | async-done | bytes 98320
  144.3 1.9 all_gather.22
  148.7 4.8 %all-to-all-start.3 = ((bf16[4,2,3072]{2,1,0:T(2,128)(2,1)}), bf16[4,2,3072]{2,1,0:T(2,128)(2,1)S(1)}, u32[]{:S(2)}, u32[]{:S(2)}) async-start(bf16[4,2,3072]{2,1,0:T(2,128)(2,1)} %reshape.271), calls=%async_computation.3 | async-start | bytes 98304 | tf_op jit(solution)/shard_map/all_to_all | solution.py:252
  153.7 5.5 %all-to-all-done.3 = bf16[4,2,3072]{2,1,0:T(2,128)(2,1)S(1)} async-done(((bf16[4,2,3072]{2,1,0:T(2,128)(2,1)}), bf16[4,2,3072]{2,1,0:T(2,128)(2,1)S(1)}, u32[]{:S(2)}, u32[]{:S(2)}) %all-to-all-start.3) | async-done | bytes 49184 | tf_op jit(solution)/shard_map/all_to_all | solution.py:252
  162.6 3.5 %all-to-all-start.4 = ((bf16[4,2,3072]{2,1,0:T(2,128)(2,1)}), bf16[4,2,3072]{2,1,0:T(2,128)(2,1)S(1)}, u32[]{:S(2)}, u32[]{:S(2)}) async-start(bf16[4,2,3072]{2,1,0:T(2,128)(2,1)} %reshape.275), calls=%async_computation.4 | async-start | bytes 98304 | tf_op jit(solution)/shard_map/all_to_all | solution.py:263
  166.3 1.2 reduce.10
  168.3 3.2 %all-to-all-done.4 = bf16[4,2,3072]{2,1,0:T(2,128)(2,1)S(1)} async-done(((bf16[4,2,3072]{2,1,0:T(2,128)(2,1)}), bf16[4,2,3072]{2,1,0:T(2,128)(2,1)S(1)}, u32[]{:S(2)}, u32[]{:S(2)}) %all-to-all-start.4) | async-done | bytes 49184 | tf_op jit(solution)/shard_map/all_to_all | solution.py:263
  172.1 3.9 %all-to-all-start.5 = ((bf16[4,2,6144]{2,1,0:T(2,128)(2,1)}), bf16[4,2,6144]{2,1,0:T(2,128)(2,1)}, u32[]{:S(2)}, u32[]{:S(2)}) async-start(bf16[4,2,6144]{2,1,0:T(2,128)(2,1)} %reshape.273), calls=%async_computation.5 | async-start | bytes 196608 | tf_op jit(solution)/shard_map/all_to_all | solution.py:270
  179.6 1.6 convert_element_type.213
  181.9 1.7 reshape.274
  183.6 1.5 reduce.5
  190.2 1.5 fusion.17
  192.6 8.3 %reduce-scatter.9.cloned.1.call-done = bf16[384,64]{1,0:T(8,128)(2,1)} async-done(((bf16[768,64]{1,0:T(8,128)(2,1)}), bf16[384,64]{1,0:T(8,128)(2,1)}) %reduce-scatter.9.cloned.1.call-update) | async-done | bytes 49168
  202.9 2.5 %psum.14 = f32[64]{0:T(128)S(1)} all-reduce(f32[64]{0:T(128)S(1)} %fusion.106), channel_id=1, replica_groups=mesh['group'=2,'seq'=4,'batch'=2,'mp'=2] {'mp'}, use_global_device_ids=true, to_apply=%region_9.0 | all-reduce | flops 64 | bytes 512 | tf_op jit(solution)/shard_map/psum | solution.py:303
  206.8 1.3 collective-permute-start.2
  208.4 4.5 %collective-permute-start.3 = (bf16[2,384]{1,0:T(2,128)(2,1)S(1)}, bf16[2,384]{1,0:T(2,128)(2,1)S(1)}, u32[]{:S(2)}, u32[]{:S(2)}) collective-permute-start(bf16[2,384]{1,0:T(2,128)(2,1)S(1)} %get-tuple-element.93), channel_id=1, source_target_pairs={{0,4},{4,8},{8,12},{1,5},{5,9},{9,13},{2,6},{6,10},{10,14},{3,7},{... | collective-permute-start | bytes 4616 | tf_op jit(solution)/shard_map/ppermute | solution.py:21
  216.2 19.2 %all-reduce.2.cloned.1.call-done = bf16[128,384]{1,0:T(8,128)(2,1)} async-done(((bf16[128,384]{1,0:T(8,128)(2,1)}), bf16[128,384]{1,0:T(8,128)(2,1)}) %all-reduce.2.cloned.1.call-update) | async-done | bytes 98320 | tf_op jit(solution)/shard_map/psum | solution.py:324
  236.5 1.7 fusion.60
  (154 shorter events, 43.7 us)
Async XLA Ops:
  7.2 13.7 %copy-start.4 = (bf16[1,128,384]{2,1,0:T(8,128)(2,1)S(1)}, bf16[1,128,384]{2,1,0:T(8,128)(2,1)}, u32[]{:S(2)}) copy-start(bf16[1,128,384]{2,1,0:T(8,128)(2,1)} %param.7) | copy-start | bytes 294916
  7.2 40.5 %all-gather.4.cloned.1.call-start = ((), (), s32[]{:S(2)}) async-start(), calls=%async_computation.8 | async-start | bytes 1843200 | tf_op jit(solution)/shard_map/all_gather | solution.py:112
  7.9 80.5 %all-gather.6.cloned.1.call-start = ((), (), s32[]{:S(2)}) async-start(), calls=%async_computation.9 | async-start | bytes 2211840 | tf_op jit(solution)/shard_map/all_gather | solution.py:133
  10.4 6.3 %collective-permute-start = (bf16[2,2,384]{2,1,0:T(2,128)(2,1)S(1)}, bf16[2,2,384]{2,1,0:T(2,128)(2,1)S(1)}, u32[]{:S(2)}, u32[]{:S(2)}) collective-permute-start(bf16[2,2,384]{2,1,0:T(2,128)(2,1)S(1)} %get-tuple-element.88), channel_id=1, source_target_pairs={{0,4},{4,8},{8,12},{1,5},{5,9},{9,13},{2,6},{6,10},{10,14},{3,7},{... | collective-permute-start | bytes 9224 | tf_op jit(solution)/shard_map/ppermute | solution.py:21
  15.4 5.5 %collective-permute-start.1 = (bf16[2,2,384]{2,1,0:T(2,128)(2,1)S(1)}, bf16[2,2,384]{2,1,0:T(2,128)(2,1)S(1)}, u32[]{:S(2)}, u32[]{:S(2)}) collective-permute-start(bf16[2,2,384]{2,1,0:T(2,128)(2,1)S(1)} %get-tuple-element.89), channel_id=1, source_target_pairs={{4,0},{8,4},{12,8},{5,1},{9,5},{13,9},{6,2},{10,6},{14,10},{7,3},{... | collective-permute-start | bytes 9224 | tf_op jit(solution)/shard_map/ppermute | solution.py:23
  47.6 2.6 %copy-start.1 = (bf16[5,384,384]{2,1,0:T(8,128)(2,1)S(1)}, bf16[5,384,384]{2,1,0:T(8,128)(2,1)}, u32[]{:S(2)}) copy-start(bf16[5,384,384]{2,1,0:T(8,128)(2,1)} %all-gather.4.cloned.1.call-done) | copy-start | bytes 4423684
  50.2 0.7 copy-start.10
  51.3 84.9 %copy-start.2 = (f32[2,128,384]{2,1,0:T(8,128)}, f32[2,128,384]{2,1,0:T(8,128)S(1)}, u32[]{:S(2)}) copy-start(f32[2,128,384]{2,1,0:T(8,128)S(1)} %get-tuple-element.95) | copy-start | bytes 1179652
  51.3 37.1 %copy-start.9 = (f32[768]{0:T(1024)S(1)}, f32[768]{0:T(1024)}, u32[]{:S(2)}) copy-start(f32[768]{0:T(1024)} %param.11) | copy-start | bytes 9220
  91.5 9.1 %all-to-all-start = ((bf16[4,2,6144]{2,1,0:T(2,128)(2,1)}), bf16[4,2,6144]{2,1,0:T(2,128)(2,1)S(1)}, u32[]{:S(2)}, u32[]{:S(2)}) async-start(bf16[4,2,6144]{2,1,0:T(2,128)(2,1)} %reshape.242), calls=%async_computation | async-start | bytes 196608 | tf_op jit(solution)/shard_map/all_to_all | solution.py:161
  100.6 9.6 %all-to-all-start.1 = ((bf16[4,2,12288]{2,1,0:T(2,128)(2,1)}), bf16[4,2,12288]{2,1,0:T(2,128)(2,1)S(1)}, u32[]{:S(2)}, u32[]{:S(2)}) async-start(bf16[4,2,12288]{2,1,0:T(2,128)(2,1)} %reshape_reshape.4), calls=%async_computation.1 | async-start | bytes 393216 | tf_op jit(solution)/shard_map/all_to_all | solution.py:162
  110.6 6.0 %copy-start.8 = (bf16[384,192]{0,1:T(8,128)(2,1)S(1)}, bf16[384,192]{0,1:T(8,128)(2,1)}, u32[]{:S(2)}) copy-start(bf16[384,192]{0,1:T(8,128)(2,1)} %param.13) | copy-start | bytes 442372
  113.2 20.2 %all-to-all-start.2 = ((bf16[4,2,6144]{2,1,0:T(2,128)(2,1)}), bf16[4,2,6144]{2,1,0:T(2,128)(2,1)S(1)}, u32[]{:S(2)}, u32[]{:S(2)}) async-start(bf16[4,2,6144]{2,1,0:T(2,128)(2,1)} %copy.103), calls=%async_computation.2 | async-start | bytes 196608 | tf_op jit(solution)/shard_map/all_to_all | solution.py:179
  116.6 26.5 %reduce-scatter.7.cloned.1.call-start = ((), (), s32[]{:S(2)}) async-start(), calls=%async_computation.11 | async-start | bytes 294912
  148.7 10.5 %all-to-all-start.3 = ((bf16[4,2,3072]{2,1,0:T(2,128)(2,1)}), bf16[4,2,3072]{2,1,0:T(2,128)(2,1)S(1)}, u32[]{:S(2)}, u32[]{:S(2)}) async-start(bf16[4,2,3072]{2,1,0:T(2,128)(2,1)} %reshape.271), calls=%async_computation.3 | async-start | bytes 98304 | tf_op jit(solution)/shard_map/all_to_all | solution.py:252
  162.6 8.9 %all-to-all-start.4 = ((bf16[4,2,3072]{2,1,0:T(2,128)(2,1)}), bf16[4,2,3072]{2,1,0:T(2,128)(2,1)S(1)}, u32[]{:S(2)}, u32[]{:S(2)}) async-start(bf16[4,2,3072]{2,1,0:T(2,128)(2,1)} %reshape.275), calls=%async_computation.4 | async-start | bytes 98304 | tf_op jit(solution)/shard_map/all_to_all | solution.py:263
  171.5 0.6 copy-start.7
  172.1 9.8 %all-to-all-start.5 = ((bf16[4,2,6144]{2,1,0:T(2,128)(2,1)}), bf16[4,2,6144]{2,1,0:T(2,128)(2,1)}, u32[]{:S(2)}, u32[]{:S(2)}) async-start(bf16[4,2,6144]{2,1,0:T(2,128)(2,1)} %reshape.273), calls=%async_computation.5 | async-start | bytes 196608 | tf_op jit(solution)/shard_map/all_to_all | solution.py:270
  176.0 14.2 %copy-start = (bf16[3,768,384]{2,1,0:T(8,128)(2,1)S(1)}, bf16[3,768,384]{2,1,0:T(8,128)(2,1)}, u32[]{:S(2)}) copy-start(bf16[3,768,384]{2,1,0:T(8,128)(2,1)} %all-gather.6.cloned.1.call-done) | copy-start | bytes 5308420
  176.1 24.8 %reduce-scatter.9.cloned.1.call-start = ((), (), s32[]{:S(2)}) async-start(), calls=%async_computation.12 | async-start | bytes 294912
  191.7 14.9 %copy-start.3 = (f32[2,128,384]{2,1,0:T(8,128)S(1)}, f32[2,128,384]{2,1,0:T(8,128)}, u32[]{:S(2)}) copy-start(f32[2,128,384]{2,1,0:T(8,128)} %copy-done.2) | copy-start | bytes 1179652
  191.7 16.4 %copy-start.6 = (f32[64,2,384]{2,1,0:T(2,128)S(1)}, f32[64,2,384]{2,1,0:T(2,128)}, u32[]{:S(2)}) copy-start(f32[64,2,384]{2,1,0:T(2,128)} %squeeze.90) | copy-start | bytes 589828
  192.6 42.9 %all-reduce.2.cloned.1.call-start = ((), (), s32[]{:S(2)}) async-start(), calls=%async_computation.10 | async-start | bytes 196608 | tf_op jit(solution)/shard_map/psum | solution.py:324
  206.8 6.4 %collective-permute-start.2 = (bf16[2,384]{1,0:T(2,128)(2,1)S(1)}, bf16[2,384]{1,0:T(2,128)(2,1)S(1)}, u32[]{:S(2)}, u32[]{:S(2)}) collective-permute-start(bf16[2,384]{1,0:T(2,128)(2,1)S(1)} %get-tuple-element.92), channel_id=1, source_target_pairs={{4,0},{8,4},{12,8},{5,1},{9,5},{13,9},{6,2},{10,6},{14,10},{7,3},{... | collective-permute-start | bytes 4616 | tf_op jit(solution)/shard_map/ppermute | solution.py:23
  208.4 5.8 %collective-permute-start.3 = (bf16[2,384]{1,0:T(2,128)(2,1)S(1)}, bf16[2,384]{1,0:T(2,128)(2,1)S(1)}, u32[]{:S(2)}, u32[]{:S(2)}) collective-permute-start(bf16[2,384]{1,0:T(2,128)(2,1)S(1)} %get-tuple-element.93), channel_id=1, source_target_pairs={{0,4},{4,8},{8,12},{1,5},{5,9},{9,13},{2,6},{6,10},{10,14},{3,7},{... | collective-permute-start | bytes 4616 | tf_op jit(solution)/shard_map/ppermute | solution.py:21
  213.4 23.1 %copy-start.5 = (f32[1,128,384]{2,1,0:T(8,128)S(1)}, f32[1,128,384]{2,1,0:T(8,128)}, u32[]{:S(2)}) copy-start(f32[1,128,384]{2,1,0:T(8,128)} %param.8) | copy-start | bytes 589828
Sparse Core Ops, SparseCore 0:
  9.6 38.0 all-gather.3
  49.2 39.1 all-gather.5
  135.6 7.4 reduce-scatter.6
  192.7 8.1 reduce-scatter.8
  215.7 19.7 all-reduce.1
where the time goes:
time: 246 us; the launch traced here: 245 us
  waiting for transfers between devices  120 us (49%)
  starting transfers between devices  34.4 us (14%)
  local copies, waits for them, and re-layouts  27.7 us (11%)
  blocking collectives  23.1 us (9%)
  between operations  14.6 us (6%)
  other arithmetic  13.9 us (6%)
  matrix products  11.3 us (5%)
    all_gather x1, waiting for transfers between devices, forward(): lax.all_gather(qkv_weight, 'seq', axis=1, tiled=True)  34.5 us
    all_gather x1, waiting for transfers between devices, forward(): piece = lax.all_gather(conv_weight, 'seq', axis=1, tiled=True)  26.7 us
    psum x1, waiting for transfers between devices, shards(): lax.psum(running.astype(jnp.bfloat16), 'mp').astype(jnp.float32)  19.2 us
    all_gather x1, blocking collectives, forward(): lax.all_gather(out_weight, 'seq', axis=1, tiled=True)  16.8 us
    unnamed x7, waiting for transfers between devices  14.9 us
    unnamed x34, local copies, waits for them, and re-layouts  9.74 us
    ppermute x2, starting transfers between devices, with_halo(): lax.ppermute(tail, axis, [(i, (i + 1) % count) for i in range(ends)])  9.49 us
    all_to_all x1, waiting for transfers between devices, forward(): lax.all_to_all(keyval_send, 'seq', split_axis=0, concat_axis=2, tiled=True)  5.54 us
  transfers between devices with their start and end apart: 15, of which 12 were waited for; matrix products, arithmetic and copies ran while one was open for 8% of the time, Pallas kernels for 0%

commit v1 on v0

--- a/solution.py
+++ b/solution.py
@@ -321,7 +321,9 @@
             piece[offset],
             preferred_element_type=jnp.float32,
         )
-    input_grad = lax.psum(running.astype(jnp.bfloat16), "mp").astype(jnp.float32)
+    input_grad = jnp.sum(lax.all_gather(running.astype(jnp.bfloat16), "mp"), axis=0).astype(
+        jnp.float32
+    )
     new_noise = noise[0] + step_size * input_grad * lax.rsqrt(
         jnp.mean(input_grad * input_grad, axis=1, keepdims=True) + epsilon
     )

time: 246 us -> 226 us (0.919)
  waiting for transfers between devices: 120 us -> 99.9 us
    psum x1 -> x0, waiting for transfers between devices: 19.2 us -> none  [shards(): lax.psum(running.astype(jnp.bfloat16), 'mp').astype(jnp.float32)]
    unnamed x7 -> x6, waiting for transfers between devices: 14.9 us -> 14.3 us
  transfers between devices with their start and end apart: 15 -> 14, of which waited for: 12 -> 11; matrix products, arithmetic and copies ran while one was open for 8% -> 9% of each run, Pallas kernels for 0% -> 0%
where the time goes in v1:
time: 226 us; the launch traced here: 224 us
  waiting for transfers between devices  99.9 us (44%)
  starting transfers between devices  34.4 us (15%)
  local copies, waits for them, and re-layouts  27.7 us (12%)
  blocking collectives  25 us (11%)
  between operations  14.6 us (6%)
  other arithmetic  12.1 us (5%)
  matrix products  10.7 us (5%)
    all_gather x1, waiting for transfers between devices, forward(): lax.all_gather(qkv_weight, 'seq', axis=1, tiled=True)  34.5 us
    all_gather x1, waiting for transfers between devices, forward(): piece = lax.all_gather(conv_weight, 'seq', axis=1, tiled=True)  26.7 us
    all_gather x1, blocking collectives, forward(): lax.all_gather(out_weight, 'seq', axis=1, tiled=True)  16.8 us
    unnamed x6, waiting for transfers between devices  14.3 us
    unnamed x34, local copies, waits for them, and re-layouts  9.74 us
    ppermute x2, starting transfers between devices, with_halo(): lax.ppermute(tail, axis, [(i, (i + 1) % count) for i in range(ends)])  9.49 us
    all_to_all x1, waiting for transfers between devices, forward(): lax.all_to_all(keyval_send, 'seq', split_axis=0, concat_axis=2, tiled=True)  5.54 us
    all_to_all x1, waiting for transfers between devices, shards(): lax.all_to_all(grad_send, 'seq', split_axis=0, concat_axis=1, tiled=True)  5.5 us
  transfers between devices with their start and end apart: 14, of which 11 were waited for; matrix products, arithmetic and copies ran while one was open for 9% of the time, Pallas kernels for 0%

profile of v1, /device:TPU:0, one launch (start us, length us, event | category | flops | bytes accessed | tf_op | source)
XLA Modules:
  0.0 224.3 jit_solution(7525956830794454648)
XLA Ops:
  10.4 4.9 %collective-permute-start = (bf16[2,2,384]{2,1,0:T(2,128)(2,1)S(1)}, bf16[2,2,384]{2,1,0:T(2,128)(2,1)S(1)}, u32[]{:S(2)}, u32[]{:S(2)}) collective-permute-start(bf16[2,2,384]{2,1,0:T(2,128)(2,1)S(1)} %get-tuple-element.88), channel_id=1, source_target_pairs={{0,4},{4,8},{8,12},{1,5},{5,9},{9,13},{2,6},{6,10},{10,14},{3,7},{... | collective-permute-start | bytes 9224 | tf_op jit(solution)/shard_map/ppermute | solution.py:21
  15.4 1.3 collective-permute-start.1
  16.7 4.2 %collective-permute-done.1 = bf16[2,2,384]{2,1,0:T(2,128)(2,1)S(1)} collective-permute-done((bf16[2,2,384]{2,1,0:T(2,128)(2,1)S(1)}, bf16[2,2,384]{2,1,0:T(2,128)(2,1)S(1)}, u32[]{:S(2)}, u32[]{:S(2)}) %collective-permute-start.1) | collective-permute-done | bytes 3104 | tf_op jit(solution)/shard_map/ppermute | solution.py:23
  20.9 26.7 %all-gather.5.cloned.1.call-done = bf16[5,384,384]{2,1,0:T(8,128)(2,1)} async-done(((bf16[5,96,384]{2,1,0:T(8,128)(2,1)}), bf16[5,384,384]{2,1,0:T(8,128)(2,1)}) %all-gather.5.cloned.1.call-update) | async-done | bytes 1474576 | tf_op jit(solution)/shard_map/all_gather | solution.py:112
  47.6 1.3 fusion.38
  49.0 1.2 fusion.42
  51.9 1.9 all-gather
  54.0 34.5 %all-gather.7.cloned.1.call-done = bf16[3,768,384]{2,1,0:T(8,128)(2,1)} async-done(((bf16[3,192,384]{2,1,0:T(8,128)(2,1)}), bf16[3,768,384]{2,1,0:T(8,128)(2,1)}) %all-gather.7.cloned.1.call-update) | async-done | bytes 1769488 | tf_op jit(solution)/shard_map/all_gather | solution.py:133
  88.5 2.0 fusion.8
  91.5 3.3 %all-to-all-start = ((bf16[4,2,6144]{2,1,0:T(2,128)(2,1)}), bf16[4,2,6144]{2,1,0:T(2,128)(2,1)S(1)}, u32[]{:S(2)}, u32[]{:S(2)}) async-start(bf16[4,2,6144]{2,1,0:T(2,128)(2,1)} %reshape.270), calls=%async_computation | async-start | bytes 196608 | tf_op jit(solution)/shard_map/all_to_all | solution.py:161
  96.3 4.3 %all-to-all-done = bf16[4,2,6144]{2,1,0:T(2,128)(2,1)S(1)} async-done(((bf16[4,2,6144]{2,1,0:T(2,128)(2,1)}), bf16[4,2,6144]{2,1,0:T(2,128)(2,1)S(1)}, u32[]{:S(2)}, u32[]{:S(2)}) %all-to-all-start) | async-done | bytes 98336 | tf_op jit(solution)/shard_map/all_to_all | solution.py:161
  100.6 3.4 %all-to-all-start.1 = ((bf16[4,2,12288]{2,1,0:T(2,128)(2,1)}), bf16[4,2,12288]{2,1,0:T(2,128)(2,1)S(1)}, u32[]{:S(2)}, u32[]{:S(2)}) async-start(bf16[4,2,12288]{2,1,0:T(2,128)(2,1)} %reshape_reshape.4), calls=%async_computation.1 | async-start | bytes 393216 | tf_op jit(solution)/shard_map/all_to_all | solution.py:162
  104.6 5.5 %all-to-all-done.1 = bf16[4,2,12288]{2,1,0:T(2,128)(2,1)S(1)} async-done(((bf16[4,2,12288]{2,1,0:T(2,128)(2,1)}), bf16[4,2,12288]{2,1,0:T(2,128)(2,1)S(1)}, u32[]{:S(2)}, u32[]{:S(2)}) %all-to-all-start.1) | async-done | bytes 196640 | tf_op jit(solution)/shard_map/all_to_all | solution.py:162
  113.2 3.3 %all-to-all-start.2 = ((bf16[4,2,6144]{2,1,0:T(2,128)(2,1)}), bf16[4,2,6144]{2,1,0:T(2,128)(2,1)S(1)}, u32[]{:S(2)}, u32[]{:S(2)}) async-start(bf16[4,2,6144]{2,1,0:T(2,128)(2,1)} %copy.103), calls=%async_computation.2 | async-start | bytes 196608 | tf_op jit(solution)/shard_map/all_to_all | solution.py:179
  116.6 16.8 %all_gather.27 = bf16[384,768]{0,1:T(8,128)(2,1)S(1)} all-gather(bf16[384,192]{0,1:T(8,128)(2,1)S(1)} %copy-done.8), channel_id=1, replica_groups=mesh['group'=2,'seq'=4,'batch'=2,'mp'=2] {'seq'}, dimensions={1}, use_global_device_ids=true | all-gather | bytes 737280 | tf_op jit(solution)/shard_map/all_gather | solution.py:188
  137.8 5.3 %reduce-scatter.7.cloned.1.call-done = bf16[384,128]{1,0:T(8,128)(2,1)} async-done(((bf16[768,128]{1,0:T(8,128)(2,1)}), bf16[384,128]{1,0:T(8,128)(2,1)}) %reduce-scatter.7.cloned.1.call-update) | async-done | bytes 98320
  144.3 1.9 all_gather.28
  148.7 4.8 %all-to-all-start.3 = ((bf16[4,2,3072]{2,1,0:T(2,128)(2,1)}), bf16[4,2,3072]{2,1,0:T(2,128)(2,1)S(1)}, u32[]{:S(2)}, u32[]{:S(2)}) async-start(bf16[4,2,3072]{2,1,0:T(2,128)(2,1)} %reshape.301), calls=%async_computation.3 | async-start | bytes 98304 | tf_op jit(solution)/shard_map/all_to_all | solution.py:252
  153.7 5.5 %all-to-all-done.3 = bf16[4,2,3072]{2,1,0:T(2,128)(2,1)S(1)} async-done(((bf16[4,2,3072]{2,1,0:T(2,128)(2,1)}), bf16[4,2,3072]{2,1,0:T(2,128)(2,1)S(1)}, u32[]{:S(2)}, u32[]{:S(2)}) %all-to-all-start.3) | async-done | bytes 49184 | tf_op jit(solution)/shard_map/all_to_all | solution.py:252
  162.6 3.5 %all-to-all-start.4 = ((bf16[4,2,3072]{2,1,0:T(2,128)(2,1)}), bf16[4,2,3072]{2,1,0:T(2,128)(2,1)S(1)}, u32[]{:S(2)}, u32[]{:S(2)}) async-start(bf16[4,2,3072]{2,1,0:T(2,128)(2,1)} %reshape.305), calls=%async_computation.4 | async-start | bytes 98304 | tf_op jit(solution)/shard_map/all_to_all | solution.py:263
  166.3 1.2 reduce.11
  168.3 3.2 %all-to-all-done.4 = bf16[4,2,3072]{2,1,0:T(2,128)(2,1)S(1)} async-done(((bf16[4,2,3072]{2,1,0:T(2,128)(2,1)}), bf16[4,2,3072]{2,1,0:T(2,128)(2,1)S(1)}, u32[]{:S(2)}, u32[]{:S(2)}) %all-to-all-start.4) | async-done | bytes 49184 | tf_op jit(solution)/shard_map/all_to_all | solution.py:263
  172.1 3.9 %all-to-all-start.5 = ((bf16[4,2,6144]{2,1,0:T(2,128)(2,1)}), bf16[4,2,6144]{2,1,0:T(2,128)(2,1)}, u32[]{:S(2)}, u32[]{:S(2)}) async-start(bf16[4,2,6144]{2,1,0:T(2,128)(2,1)} %reshape.303), calls=%async_computation.5 | async-start | bytes 196608 | tf_op jit(solution)/shard_map/all_to_all | solution.py:270
  179.6 1.6 convert_element_type.227
  181.9 1.7 reshape.304
  183.6 1.5 reduce.6
  190.2 1.5 fusion.17
  193.2 7.7 %reduce-scatter.9.cloned.1.call-done = bf16[384,64]{1,0:T(8,128)(2,1)} async-done(((bf16[768,64]{1,0:T(8,128)(2,1)}), bf16[384,64]{1,0:T(8,128)(2,1)}) %reduce-scatter.9.cloned.1.call-update) | async-done | bytes 49168
  202.9 2.5 %psum.7 = f32[64]{0:T(128)S(1)} all-reduce(f32[64]{0:T(128)S(1)} %fusion.106), channel_id=1, replica_groups=mesh['group'=2,'seq'=4,'batch'=2,'mp'=2] {'mp'}, use_global_device_ids=true, to_apply=%region_9.0 | all-reduce | flops 64 | bytes 512 | tf_op jit(solution)/shard_map/psum | solution.py:303
  206.8 1.3 collective-permute-start.2
  208.4 4.5 %collective-permute-start.3 = (bf16[2,384]{1,0:T(2,128)(2,1)S(1)}, bf16[2,384]{1,0:T(2,128)(2,1)S(1)}, u32[]{:S(2)}, u32[]{:S(2)}) collective-permute-start(bf16[2,384]{1,0:T(2,128)(2,1)S(1)} %get-tuple-element.93), channel_id=1, source_target_pairs={{0,4},{4,8},{8,12},{1,5},{5,9},{9,13},{2,6},{6,10},{10,14},{3,7},{... | collective-permute-start | bytes 4616 | tf_op jit(solution)/shard_map/ppermute | solution.py:21
  214.9 1.9 all-gather.1
  (153 shorter events, 41.6 us)
Async XLA Ops:
  7.2 13.7 %copy-start.4 = (bf16[1,128,384]{2,1,0:T(8,128)(2,1)S(1)}, bf16[1,128,384]{2,1,0:T(8,128)(2,1)}, u32[]{:S(2)}) copy-start(bf16[1,128,384]{2,1,0:T(8,128)(2,1)} %param.7) | copy-start | bytes 294916
  7.2 40.5 %all-gather.5.cloned.1.call-start = ((), (), s32[]{:S(2)}) async-start(), calls=%async_computation.8 | async-start | bytes 1843200 | tf_op jit(solution)/shard_map/all_gather | solution.py:112
  7.9 80.5 %all-gather.7.cloned.1.call-start = ((), (), s32[]{:S(2)}) async-start(), calls=%async_computation.9 | async-start | bytes 2211840 | tf_op jit(solution)/shard_map/all_gather | solution.py:133
  10.4 6.3 %collective-permute-start = (bf16[2,2,384]{2,1,0:T(2,128)(2,1)S(1)}, bf16[2,2,384]{2,1,0:T(2,128)(2,1)S(1)}, u32[]{:S(2)}, u32[]{:S(2)}) collective-permute-start(bf16[2,2,384]{2,1,0:T(2,128)(2,1)S(1)} %get-tuple-element.88), channel_id=1, source_target_pairs={{0,4},{4,8},{8,12},{1,5},{5,9},{9,13},{2,6},{6,10},{10,14},{3,7},{... | collective-permute-start | bytes 9224 | tf_op jit(solution)/shard_map/ppermute | solution.py:21
  15.4 5.5 %collective-permute-start.1 = (bf16[2,2,384]{2,1,0:T(2,128)(2,1)S(1)}, bf16[2,2,384]{2,1,0:T(2,128)(2,1)S(1)}, u32[]{:S(2)}, u32[]{:S(2)}) collective-permute-start(bf16[2,2,384]{2,1,0:T(2,128)(2,1)S(1)} %get-tuple-element.89), channel_id=1, source_target_pairs={{4,0},{8,4},{12,8},{5,1},{9,5},{13,9},{6,2},{10,6},{14,10},{7,3},{... | collective-permute-start | bytes 9224 | tf_op jit(solution)/shard_map/ppermute | solution.py:23
  47.6 2.6 %copy-start.1 = (bf16[5,384,384]{2,1,0:T(8,128)(2,1)S(1)}, bf16[5,384,384]{2,1,0:T(8,128)(2,1)}, u32[]{:S(2)}) copy-start(bf16[5,384,384]{2,1,0:T(8,128)(2,1)} %all-gather.5.cloned.1.call-done) | copy-start | bytes 4423684
  50.2 0.7 copy-start.10
  51.3 84.9 %copy-start.2 = (f32[2,128,384]{2,1,0:T(8,128)}, f32[2,128,384]{2,1,0:T(8,128)S(1)}, u32[]{:S(2)}) copy-start(f32[2,128,384]{2,1,0:T(8,128)S(1)} %get-tuple-element.95) | copy-start | bytes 1179652
  51.3 37.1 %copy-start.9 = (f32[768]{0:T(1024)S(1)}, f32[768]{0:T(1024)}, u32[]{:S(2)}) copy-start(f32[768]{0:T(1024)} %param.11) | copy-start | bytes 9220
  91.5 9.1 %all-to-all-start = ((bf16[4,2,6144]{2,1,0:T(2,128)(2,1)}), bf16[4,2,6144]{2,1,0:T(2,128)(2,1)S(1)}, u32[]{:S(2)}, u32[]{:S(2)}) async-start(bf16[4,2,6144]{2,1,0:T(2,128)(2,1)} %reshape.270), calls=%async_computation | async-start | bytes 196608 | tf_op jit(solution)/shard_map/all_to_all | solution.py:161
  100.6 9.6 %all-to-all-start.1 = ((bf16[4,2,12288]{2,1,0:T(2,128)(2,1)}), bf16[4,2,12288]{2,1,0:T(2,128)(2,1)S(1)}, u32[]{:S(2)}, u32[]{:S(2)}) async-start(bf16[4,2,12288]{2,1,0:T(2,128)(2,1)} %reshape_reshape.4), calls=%async_computation.1 | async-start | bytes 393216 | tf_op jit(solution)/shard_map/all_to_all | solution.py:162
  110.6 6.0 %copy-start.8 = (bf16[384,192]{0,1:T(8,128)(2,1)S(1)}, bf16[384,192]{0,1:T(8,128)(2,1)}, u32[]{:S(2)}) copy-start(bf16[384,192]{0,1:T(8,128)(2,1)} %param.13) | copy-start | bytes 442372
  113.2 20.2 %all-to-all-start.2 = ((bf16[4,2,6144]{2,1,0:T(2,128)(2,1)}), bf16[4,2,6144]{2,1,0:T(2,128)(2,1)S(1)}, u32[]{:S(2)}, u32[]{:S(2)}) async-start(bf16[4,2,6144]{2,1,0:T(2,128)(2,1)} %copy.103), calls=%async_computation.2 | async-start | bytes 196608 | tf_op jit(solution)/shard_map/all_to_all | solution.py:179
  116.6 26.5 %reduce-scatter.7.cloned.1.call-start = ((), (), s32[]{:S(2)}) async-start(), calls=%async_computation.10 | async-start | bytes 294912
  148.7 10.5 %all-to-all-start.3 = ((bf16[4,2,3072]{2,1,0:T(2,128)(2,1)}), bf16[4,2,3072]{2,1,0:T(2,128)(2,1)S(1)}, u32[]{:S(2)}, u32[]{:S(2)}) async-start(bf16[4,2,3072]{2,1,0:T(2,128)(2,1)} %reshape.301), calls=%async_computation.3 | async-start | bytes 98304 | tf_op jit(solution)/shard_map/all_to_all | solution.py:252
  162.6 8.9 %all-to-all-start.4 = ((bf16[4,2,3072]{2,1,0:T(2,128)(2,1)}), bf16[4,2,3072]{2,1,0:T(2,128)(2,1)S(1)}, u32[]{:S(2)}, u32[]{:S(2)}) async-start(bf16[4,2,3072]{2,1,0:T(2,128)(2,1)} %reshape.305), calls=%async_computation.4 | async-start | bytes 98304 | tf_op jit(solution)/shard_map/all_to_all | solution.py:263
  171.5 0.6 copy-start.7
  172.1 9.8 %all-to-all-start.5 = ((bf16[4,2,6144]{2,1,0:T(2,128)(2,1)}), bf16[4,2,6144]{2,1,0:T(2,128)(2,1)}, u32[]{:S(2)}, u32[]{:S(2)}) async-start(bf16[4,2,6144]{2,1,0:T(2,128)(2,1)} %reshape.303), calls=%async_computation.5 | async-start | bytes 196608 | tf_op jit(solution)/shard_map/all_to_all | solution.py:270
  176.0 14.2 %copy-start = (bf16[3,768,384]{2,1,0:T(8,128)(2,1)S(1)}, bf16[3,768,384]{2,1,0:T(8,128)(2,1)}, u32[]{:S(2)}) copy-start(bf16[3,768,384]{2,1,0:T(8,128)(2,1)} %all-gather.7.cloned.1.call-done) | copy-start | bytes 5308420
  176.1 24.8 %reduce-scatter.9.cloned.1.call-start = ((), (), s32[]{:S(2)}) async-start(), calls=%async_computation.11 | async-start | bytes 294912
  191.7 14.9 %copy-start.3 = (f32[2,128,384]{2,1,0:T(8,128)S(1)}, f32[2,128,384]{2,1,0:T(8,128)}, u32[]{:S(2)}) copy-start(f32[2,128,384]{2,1,0:T(8,128)} %copy-done.2) | copy-start | bytes 1179652
  191.7 16.4 %copy-start.6 = (f32[64,2,384]{2,1,0:T(2,128)S(1)}, f32[64,2,384]{2,1,0:T(2,128)}, u32[]{:S(2)}) copy-start(f32[64,2,384]{2,1,0:T(2,128)} %squeeze.87) | copy-start | bytes 589828
  206.8 6.4 %collective-permute-start.2 = (bf16[2,384]{1,0:T(2,128)(2,1)S(1)}, bf16[2,384]{1,0:T(2,128)(2,1)S(1)}, u32[]{:S(2)}, u32[]{:S(2)}) collective-permute-start(bf16[2,384]{1,0:T(2,128)(2,1)S(1)} %get-tuple-element.92), channel_id=1, source_target_pairs={{4,0},{8,4},{12,8},{5,1},{9,5},{13,9},{6,2},{10,6},{14,10},{7,3},{... | collective-permute-start | bytes 4616 | tf_op jit(solution)/shard_map/ppermute | solution.py:23
  208.4 5.8 %collective-permute-start.3 = (bf16[2,384]{1,0:T(2,128)(2,1)S(1)}, bf16[2,384]{1,0:T(2,128)(2,1)S(1)}, u32[]{:S(2)}, u32[]{:S(2)}) collective-permute-start(bf16[2,384]{1,0:T(2,128)(2,1)S(1)} %get-tuple-element.93), channel_id=1, source_target_pairs={{0,4},{4,8},{8,12},{1,5},{5,9},{9,13},{2,6},{6,10},{10,14},{3,7},{... | collective-permute-start | bytes 4616 | tf_op jit(solution)/shard_map/ppermute | solution.py:21
  213.4 3.6 %copy-start.5 = (f32[1,128,384]{2,1,0:T(8,128)S(1)}, f32[1,128,384]{2,1,0:T(8,128)}, u32[]{:S(2)}) copy-start(f32[1,128,384]{2,1,0:T(8,128)} %param.8) | copy-start | bytes 589828
Sparse Core Ops, SparseCore 0:
  9.6 38.0 all-gather.4
  49.2 39.1 all-gather.6
  135.6 7.4 reduce-scatter.6
  192.7 8.1 reduce-scatter.8
